TPU v7x, 32 devices: a whole 2x2x4 slice. The times are simulated.
32 devices in a mesh: req: 4 (over z), ctx: 8 (over y, x, core).
Axes of the slice: x: 2, y: 2, z: 4, core: 2. Of those that a mesh axis runs over, the one named last changes fastest.
Arguments:
- hidden_in: bfloat16 [4096, 2048], P(('req', 'ctx')), may hold values from -3 to 3
- queries: bfloat16 [4096, 1024], P(('req', 'ctx')), may hold values from -10 to 10
- span_keys: bfloat16 [4096, 1024], P(('req', 'ctx')), may hold values from -10 to 10
- span_values: bfloat16 [4096, 1024], P(('req', 'ctx')), may hold values from -6 to 6
- cache_keys: bfloat16 [6144, 1024], P(('req', 'ctx')), may hold values from -6 to 6
- cache_values: bfloat16 [6144, 1024], P(('req', 'ctx')), may hold values from -6 to 6
- cache_lengths: int32 [4], replicated, may hold values from 0 to 1536, as said below
- slot_request: int32 [4], replicated, may hold values from 0 to 3, each once
- out_weight: bfloat16 [1024, 2048], replicated, may hold values from -1.5 to 1.5
- norm_gain: float32 [2048], replicated, may hold values from 0.1 to 1.9
- expert_ids: int32 [4096, 8], P(('req', 'ctx')), may hold values from 0 to 15, all different within a row; in each aligned block of 128 rows (0 to 127, 128 to 255, ...) at most 128 rows name the same one
- expert_gates: float32 [4096, 8], P(('req', 'ctx')), may hold values from 0.05 to 0.5
- gate_proj: bfloat16 [16, 2048, 512], P('ctx'), may hold values from -0.125 to 0.125
- up_proj: bfloat16 [16, 2048, 512], P('ctx'), may hold values from -0.125 to 0.125
- down_proj: bfloat16 [16, 512, 2048], P('ctx'), may hold values from -0.25 to 0.25
Outputs:
- layer_out: bfloat16 [4096, 2048], P(('req', 'ctx'))
Inputs may be any that keep to these rules, and one draw needn't show every extreme that they name: `cache_lengths`: some request has exactly 1536 cached positions.
All inputs are finite; a program needn't handle non-finite values.
Results may differ from a plain program's by a relative error of at most 0.015.
Values may be sent and summed in bfloat16 or wider, within the bound.
No kernel may reach another device: no remote copies, remote signals or barrier semaphores. Data moves between devices by JAX's collectives and lax.ppermute only.
A program may use at most 192 MiB of HBM per device.

v0:
```python
import math

import jax
import jax.numpy as jnp
from jax import lax
from jax.sharding import PartitionSpec as P

HEAD_DIM = 128


def on_device(
    hidden_in,
    queries,
    span_keys,
    span_values,
    cache_keys,
    cache_values,
    cache_lengths,
    slot_request,
    out_weight,
    norm_gain,
    expert_ids,
    expert_gates,
    gate_proj,
    up_proj,
    down_proj,
):
    token_count, feature_width = hidden_in.shape
    column_count = queries.shape[1]
    head_count = column_count // HEAD_DIM
    cached_rows = cache_keys.shape[0]
    ctx_count = lax.axis_size("ctx")
    slot_place = lax.axis_index("req")
    slot_count = slot_request.shape[0]
    slot_range = jnp.arange(slot_count, dtype=jnp.int32)
    request = jnp.sum(jnp.where(slot_range == slot_place, slot_request, 0))
    length = jnp.sum(jnp.where(slot_range == request, cache_lengths, 0))
    key_block = jnp.concatenate([span_keys, cache_keys], 0)
    value_block = jnp.concatenate([span_values, cache_values], 0)
    block_rows = token_count + cached_rows
    scaling = 1.0 / math.sqrt(HEAD_DIM)
    query_heads = queries.reshape(token_count, head_count, HEAD_DIM)
    best = jnp.full((head_count, token_count), -1e30, jnp.float32)
    piece_keys = lax.all_gather(key_block, "ctx", axis=0, tiled=True)
    piece_values = lax.all_gather(value_block, "ctx", axis=0, tiled=True)
    piece_rows = piece_keys.shape[0]
    index = jnp.arange(piece_rows, dtype=jnp.int32)
    owner = index // block_rows
    within = index % block_rows
    usable = (within < token_count) | (owner * cached_rows + within - token_count < length)
    scores = (
        jnp.einsum(
            "thd,phd->htp",
            query_heads,
            piece_keys.reshape(piece_rows, head_count, HEAD_DIM),
            preferred_element_type=jnp.float32,
        )
        * scaling
    )
    scores = jnp.where(usable[None, None, :], scores, -1e30)
    new_best = jnp.maximum(best, jnp.max(scores, axis=2))
    weights = jnp.where(usable[None, None, :], jnp.exp(scores - new_best[:, :, None]), 0.0)
    total = jnp.sum(weights, axis=2)
    accum = jnp.einsum(
        "htp,phd->htd",
        weights.astype(jnp.bfloat16),
        piece_values.reshape(piece_rows, head_count, HEAD_DIM),
        preferred_element_type=jnp.float32,
    )
    best, total, accum = (new_best, total, accum)
    attended = (
        (accum / total[:, :, None])
        .transpose(1, 0, 2)
        .reshape(token_count, column_count)
        .astype(jnp.bfloat16)
    )
    residual = hidden_in.astype(jnp.float32) + jnp.dot(
        attended, out_weight, preferred_element_type=jnp.float32
    )
    mean_square = jnp.mean(residual * residual, axis=1, keepdims=True)
    normed = (residual * lax.rsqrt(mean_square + 1e-06) * norm_gain).astype(jnp.bfloat16)
    chosen_count = expert_ids.shape[1]
    local_experts = gate_proj.shape[0]
    experts_all = local_experts * ctx_count
    capacity = 2 * token_count * chosen_count // experts_all
    slot_total = experts_all * capacity
    flat_ids = expert_ids.reshape(-1)
    onehot = (flat_ids[:, None] == jnp.arange(experts_all, dtype=jnp.int32)[None, :]).astype(
        jnp.int32
    )
    ranking = jnp.sum((jnp.cumsum(onehot, axis=0) - 1) * onehot, axis=1)
    target = flat_ids * capacity + ranking
    source_row = jnp.arange(token_count * chosen_count, dtype=jnp.int32) // chosen_count
    slot_row = jnp.zeros((slot_total,), jnp.int32).at[target].set(source_row)
    slot_used = jnp.zeros((slot_total,), jnp.bool_).at[target].set(True)
    outgoing = jnp.where(slot_used[:, None], normed[slot_row], jnp.zeros((), jnp.bfloat16))
    outgoing = outgoing.reshape(ctx_count, local_experts, capacity, feature_width)
    batch = lax.all_to_all(outgoing, "ctx", split_axis=0, concat_axis=0, tiled=True)
    gate_val = jnp.einsum("sjcd,jdf->sjcf", batch, gate_proj, preferred_element_type=jnp.float32)
    up_val = jnp.einsum("sjcd,jdf->sjcf", batch, up_proj, preferred_element_type=jnp.float32)
    activated = (jax.nn.silu(gate_val) * up_val).astype(jnp.bfloat16)
    computed = jnp.einsum(
        "sjcf,jfd->sjcd", activated, down_proj, preferred_element_type=jnp.float32
    ).astype(jnp.bfloat16)
    returned = lax.all_to_all(computed, "ctx", split_axis=0, concat_axis=0, tiled=True).reshape(
        slot_total, feature_width
    )
    picked = returned[target].reshape(token_count, chosen_count, feature_width)
    mixed = residual
    for choice_index in range(chosen_count):
        mixed = mixed + expert_gates[:, choice_index : choice_index + 1] * picked[
            :, choice_index, :
        ].astype(jnp.float32)
    final = mixed.astype(jnp.bfloat16)
    source_slot = jnp.sum(jnp.where(slot_request == slot_place, slot_range, 0))
    piece = lax.all_gather(final, "req", axis=0, tiled=True)
    piece_rows = piece.shape[0]
    offset = source_slot * token_count
    inside = (offset >= 0) & (offset + token_count <= piece_rows)
    portion = lax.dynamic_slice_in_dim(
        piece, jnp.clip(offset, 0, piece_rows - token_count), token_count, 0
    )
    return jnp.where(inside, portion, jnp.zeros_like(final))


def solution(mesh):
    return jax.shard_map(
        on_device,
        mesh=mesh,
        in_specs=(
            P(("req", "ctx"), None),
            P(("req", "ctx"), None),
            P(("req", "ctx"), None),
            P(("req", "ctx"), None),
            P(("req", "ctx"), None),
            P(("req", "ctx"), None),
            P(),
            P(),
            P(),
            P(),
            P(("req", "ctx"), None),
            P(("req", "ctx"), None),
            P("ctx", None, None),
            P("ctx", None, None),
            P("ctx", None, None),
        ),
        out_specs=P(("req", "ctx"), None),
        check_vma=False,
    )
```

profile of v0, /device:TPU:0, one launch (start us, length us, event | category | flops | bytes accessed | tf_op | source)
XLA Modules:
  0.0 456.1 jit_solution(1173514984917608593)
XLA Ops:
  6.5 2.0 pad_maximum_fusion.1
  8.6 1.9 pad_maximum_fusion
  10.6 0.8 copy.49
  11.6 4.5 reduce-window.6
  17.5 4.3 scatter_custom_fusion.1
  21.8 4.5 scatter_custom_fusion
  26.4 1.3 fusion.71
  27.7 2.0 fusion.73
  29.7 0.7 fusion.62
  30.4 22.7 %all-gather.4.cloned.1.call-done = bf16[2560,1024]{1,0:T(8,128)(2,1)} async-done(((bf16[320,1024]{1,0:T(8,128)(2,1)}), bf16[2560,1024]{1,0:T(8,128)(2,1)}) %all-gather.4.cloned.1.call-update) | async-done | bytes 5242896 | tf_op jit(solution)/shard_map/all_gather | solution.py:44
  53.1 7.7 %copy.43 = bf16[2560,1024]{0,1:T(8,128)(2,1)} copy(bf16[2560,1024]{1,0:T(8,128)(2,1)} %all-gather.4.cloned.1.call-done) | data formatting | bytes 10485760 | tf_op jit(solution)/shard_map/all_gather | solution.py:44
  60.8 6.0 %bitcast_reduce_fusion = (f32[8,128]{1,0:T(8,128)S(1)}, f32[8,2560,128]{2,1,0:T(8,128)S(1)}) fusion(pred[2560]{0:T(1024)(128)(4,1)S(1)} %fusion.62, bf16[2560,8,128]{0,2,1:T(8,128)(2,1)} %bitcast.158, bf16[128,1024]{1,0:T(8,128)(2,1)S(1)} %copy-done), kind=kOutput, calls=%fused_computation.5 | convolution fusion | flops 678951936 | bytes 15997440 | tf_op jit(solution)/shard_map/thd,phd->htp/dot_general | solution.py:52
  66.8 4.0 copy-done.2
  70.8 3.4 fusion.6
  74.1 22.0 %all-gather.6.cloned.1.call-done = bf16[2560,1024]{1,0:T(8,128)(2,1)} async-done(((bf16[320,1024]{1,0:T(8,128)(2,1)}), bf16[2560,1024]{1,0:T(8,128)(2,1)}) %all-gather.6.cloned.1.call-update) | async-done | bytes 5242896 | tf_op jit(solution)/shard_map/all_gather | solution.py:45
  96.1 7.9 %copy.46 = bf16[2560,1024]{0,1:T(8,128)(2,1)} copy(bf16[2560,1024]{1,0:T(8,128)(2,1)} %all-gather.6.cloned.1.call-done) | data formatting | bytes 10485760 | tf_op jit(solution)/shard_map/all_gather | solution.py:45
  104.1 8.1 %fusion.43 = bf16[128,8,128]{0,2,1:T(8,128)(2,1)S(1)} fusion(bf16[2560,8,128]{0,2,1:T(8,128)(2,1)} %bitcast.161, f32[8,2560,128]{2,1,0:T(8,128)} %copy-done.2, f32[8,128]{1,0:T(8,128)S(1)} %broadcast_maximum_fusion, pred[2560]{0:T(1024)(128)(4,1)S(1)} %fusion.62, f32[128,8]{0,1:T(8,128)S(1)} %bitcast.169), kind=kOutput, calls=%fused_computation.53 | convolution fusion | flops 684457984 | bytes 16001536 | tf_op jit(solution)/shard_map/htp,phd->htd/dot_general | solution.py:64
  112.2 0.8 multiply_reduce_fusion
  113.2 11.0 %gather_fusion = bf16[2048,2048]{1,0:T(8,128)(2,1)} fusion(bf16[128,2048]{1,0:T(8,128)(2,1)S(1)} %multiply_convert_fusion, s32[2048]{0:T(1024)S(1)} %fusion.63), kind=kCustom, calls=%fused_computation | custom fusion | bytes 16785408 | tf_op jit(solution)/shard_map/gather | solution.py:96
  124.2 7.2 %broadcast_select_fusion = bf16[8,2,128,2048]{3,2,1,0:T(8,128)(2,1)} fusion(bf16[8,2,128,2048]{3,2,1,0:T(8,128)(2,1)} %bitcast.160, pred[8,2,128]{2,1,0:T(4,128)(4,1)S(1)} %broadcast_in_dim.74), kind=kLoop, calls=%fused_computation.10 | loop fusion | flops 4194304 | bytes 16779264 | tf_op jit(solution)/shard_map/jit(_where)/select_n | solution.py:96
  131.4 98.1 %all_to_all.10 = bf16[8,2,128,2048]{3,2,1,0:T(8,128)(2,1)S(1)} all-to-all(bf16[8,2,128,2048]{3,2,1,0:T(8,128)(2,1)} %broadcast_select_fusion), channel_id=1, replica_groups=mesh['req'=4,'ctx'=8] {'ctx'}, dimensions={0} | all-to-all | bytes 16777216 | tf_op jit(solution)/shard_map/all_to_all | solution.py:98
  229.5 3.2 copy-done.3
  232.7 6.0 %fusion.4 = f32[2,8,128,512]{3,2,1,0:T(8,128)} fusion(bf16[8,2,128,2048]{3,2,1,0:T(8,128)(2,1)S(1)} %all_to_all.10, bf16[2,2048,512]{2,1,0:T(8,128)(2,1)S(1)} %copy-done.8), kind=kOutput, calls=%fused_computation.13 | convolution fusion | flops 4294967296 | bytes 16777216 | tf_op jit(solution)/shard_map/sjcd,jdf->sjcf/dot_general | solution.py:99
  238.7 15.3 %convert_bitcast_fusion = bf16[8,2,128,2048]{3,2,0,1:T(8,128)(2,1)} fusion(bf16[2,512,2048]{2,1,0:T(8,128)(2,1)} %param.29, f32[2,8,128,512]{3,2,1,0:T(8,128)} %fusion.4, bf16[2,2048,512]{2,1,0:T(8,128)(2,1)} %param.28, bf16[8,2,128,2048]{3,2,1,0:T(8,128)(2,1)} %copy-done.3), kind=kOutput, calls=%fused_computation.9 | convolution fusion | flops 8600420352 | bytes 29360128 | tf_op jit(solution)/shard_map/sjcf,jfd->sjcd/dot_general | solution.py:102
  254.0 8.3 %copy.55 = bf16[8,2,128,2048]{3,2,1,0:T(8,128)(2,1)} copy(bf16[8,2,128,2048]{3,2,0,1:T(8,128)(2,1)} %convert_bitcast_fusion) | data formatting | bytes 16777216 | tf_op jit(solution)/shard_map/convert_element_type | solution.py:104
  262.2 5.1 %all-to-all-start.1 = ((bf16[8,2,128,2048]{3,2,1,0:T(8,128)(2,1)}), bf16[8,2,128,2048]{3,2,1,0:T(8,128)(2,1)}, u32[]{:S(2)}, u32[]{:S(2)}) async-start(bf16[8,2,128,2048]{3,2,1,0:T(8,128)(2,1)} %copy.55), calls=%async_computation.1 | async-start | bytes 16777216 | tf_op jit(solution)/shard_map/all_to_all | solution.py:105
  267.7 93.7 %all-to-all-done.1 = bf16[8,2,128,2048]{3,2,1,0:T(8,128)(2,1)} async-done(((bf16[8,2,128,2048]{3,2,1,0:T(8,128)(2,1)}), bf16[8,2,128,2048]{3,2,1,0:T(8,128)(2,1)}, u32[]{:S(2)}, u32[]{:S(2)}) %all-to-all-start.1) | async-done | bytes 8388640 | tf_op jit(solution)/shard_map/all_to_all | solution.py:105
  361.4 13.3 %gather_fusion.1 = bf16[1024,2048]{1,0:T(8,128)(2,1)} fusion(bf16[2048,2048]{1,0:T(8,128)(2,1)} %bitcast.21, s32[1024]{0:T(1024)S(1)} %broadcast_clamp_fusion), kind=kCustom, calls=%fused_computation.1 | custom fusion | bytes 8392704 | tf_op jit(solution)/shard_map/gather | solution.py:108
  374.7 22.2 %fusion.78 = (bf16[128,1,2048]{2,1,0:T(2,128)(2,1)S(1)}, bf16[128,1,2048]{2,1,0:T(2,128)(2,1)S(1)}, bf16[128,1,2048]{2,1,0:T(2,128)(2,1)S(1)}, bf16[128,1,2048]{...) fusion(bf16[128,8,2048]{2,1,0:T(8,128)(2,1)} %bitcast.159), kind=kLoop, calls=%fused_computation.127 | loop fusion | bytes 8388608 | tf_op jit(solution)/shard_map/slice | solution.py:111
  396.9 5.5 %fusion.32 = bf16[128,2048]{1,0:T(8,128)(2,1)} fusion(f32[128,2048]{1,0:T(8,128)S(1)} %get-tuple-element.26, bf16[128,1,2048]{2,1,0:T(2,128)(2,1)S(1)} %get-tuple-element.14, bf16[128,1,2048]{2,1,0:T(2,128)(2,1)S(1)} %get-tuple-element.8, bf16[128,1,2048]{2,1,0:T(2,128)(2,1)S(1)} %get-tuple-element.9, bf16[128,1,2048]{2,1,0:T(2,128)(2,1)S(1)} %get-tuple-element.10, ...), kind=kLoop, calls=%fused_computation.35 | loop fusion | flops 6553600 | bytes 5771264 | tf_op jit(solution)/shard_map/convert_element_type | solution.py:114
  403.0 44.6 %all-gather.8.cloned.1.call-done = bf16[512,2048]{1,0:T(8,128)(2,1)} async-done(((bf16[128,2048]{1,0:T(8,128)(2,1)}), bf16[512,2048]{1,0:T(8,128)(2,1)}) %all-gather.8.cloned.1.call-update) | async-done | bytes 2097168 | tf_op jit(solution)/shard_map/all_gather | solution.py:116
  447.6 2.0 dynamic-slice_select_fusion
  (45 shorter events, 2.2 us)
Async XLA Ops:
  6.5 54.3 %copy-start = (bf16[128,1024]{1,0:T(8,128)(2,1)S(1)}, bf16[128,1024]{1,0:T(8,128)(2,1)}, u32[]{:S(2)}) copy-start(bf16[128,1024]{1,0:T(8,128)(2,1)} %param.16) | copy-start | bytes 786436
  6.5 46.5 %all-gather.4.cloned.1.call-start = ((), (), s32[]{:S(2)}) async-start(), calls=%async_computation.2 | async-start | bytes 5898240 | tf_op jit(solution)/shard_map/all_gather | solution.py:44
  8.6 87.6 %all-gather.6.cloned.1.call-start = ((), (), s32[]{:S(2)}) async-start(), calls=%async_computation.3 | async-start | bytes 5898240 | tf_op jit(solution)/shard_map/all_gather | solution.py:45
  66.8 4.0 copy-start.2
  104.1 8.1 %copy-start.4 = (bf16[1024,2048]{1,0:T(8,128)(2,1)S(1)}, bf16[1024,2048]{1,0:T(8,128)(2,1)}, u32[]{:S(2)}) copy-start(bf16[1024,2048]{1,0:T(8,128)(2,1)} %param.23) | copy-start | bytes 12582916
  104.1 8.1 %copy-start.5 = (bf16[128,2048]{1,0:T(8,128)(2,1)S(1)}, bf16[128,2048]{1,0:T(8,128)(2,1)}, u32[]{:S(2)}) copy-start(bf16[128,2048]{1,0:T(8,128)(2,1)} %param.15) | copy-start | bytes 1572868
  112.2 0.9 copy-start.6
  131.4 101.3 %copy-start.8 = (bf16[2,2048,512]{2,1,0:T(8,128)(2,1)S(1)}, bf16[2,2048,512]{2,1,0:T(8,128)(2,1)}, u32[]{:S(2)}) copy-start(bf16[2,2048,512]{2,1,0:T(8,128)(2,1)} %param.27) | copy-start | bytes 12582916
  229.5 3.2 copy-start.3
  262.2 5.4 %copy-start.7 = (f32[128,8]{0,1:T(8,128)S(1)}, f32[128,8]{0,1:T(8,128)}, u32[]{:S(2)}) copy-start(f32[128,8]{0,1:T(8,128)} %param.26) | copy-start | bytes 12292
  262.2 99.2 %all-to-all-start.1 = ((bf16[8,2,128,2048]{3,2,1,0:T(8,128)(2,1)}), bf16[8,2,128,2048]{3,2,1,0:T(8,128)(2,1)}, u32[]{:S(2)}, u32[]{:S(2)}) async-start(bf16[8,2,128,2048]{3,2,1,0:T(8,128)(2,1)} %copy.55), calls=%async_computation.1 | async-start | bytes 16777216 | tf_op jit(solution)/shard_map/all_to_all | solution.py:105
  267.3 180.2 %all-gather.8.cloned.1.call-start = ((), (), s32[]{:S(2)}) async-start(), calls=%async_computation.4 | async-start | bytes 2621440 | tf_op jit(solution)/shard_map/all_gather | solution.py:116
  396.8 52.7 %copy-start.1 = (bf16[128,1024]{1,0:T(8,128)(2,1)S(1)}, bf16[128,1024]{1,0:T(8,128)(2,1)}, u32[]{:S(2)}) copy-start(bf16[128,1024]{1,0:T(8,128)(2,1)} %param.16) | copy-start | bytes 786436
Sparse Core Ops, SparseCore 0:
  9.2 43.8 all-gather.3
  55.0 41.1 all-gather.5
  402.5 45.0 all-gather.7
where the time goes:
time: 457 us; the launch traced here: 456 us
  waiting for transfers between devices  183 us (40%)
  blocking collectives  98.1 us (21%)
  local copies, waits for them, and re-layouts  87.9 us (19%)
  matrix products  36.1 us (8%)
  other arithmetic  31.6 us (7%)
  between operations  14 us (3%)
  starting transfers between devices  5.44 us (1%)
    all_to_all x1, blocking collectives, on_device(): lax.all_to_all(outgoing, 'ctx', split_axis=0, concat_axis=0, tiled=True)  98.1 us
    all_to_all x1, waiting for transfers between devices, on_device(): lax.all_to_all(computed, 'ctx', split_axis=0, concat_axis=0, tiled=True)  93.7 us
    all_gather x1, waiting for transfers between devices, on_device(): piece = lax.all_gather(final, 'req', axis=0, tiled=True)  44.6 us
    all_gather x1, waiting for transfers between devices, on_device(): piece_keys = lax.all_gather(key_block, 'ctx', axis=0, tiled=True)  22.7 us
    slice x1, local copies, waits for them, and re-layouts, on_device(): picked[:, choice_index, :].astype(jnp.float32)  22.2 us
    all_gather x1, waiting for transfers between devices, on_device(): piece_values = lax.all_gather(value_block, 'ctx', axis=0, tiled=True)  22 us
    dot_general x1, matrix products, on_device(): jnp.einsum('sjcf,jfd->sjcd', activated, down_proj, preferred_element_type...  15.3 us
    gather x1, local copies, waits for them, and re-layouts, on_device(): picked = returned[target].reshape(token_count, chosen_count, feature_width)  13.3 us
  transfers between devices with their start and end apart: 4, of which 4 were waited for; matrix products, arithmetic and copies ran while one was open for 8% of the time, Pallas kernels for 0%

commit v1 on v0

v1 whole, which is shorter than its diff:
```python
import math

import jax
import jax.numpy as jnp
from jax import lax
from jax.sharding import PartitionSpec as P

HEAD_DIM = 128


def attend_gathered(queries, span_keys, span_values, cache_keys, cache_values, length):
    token_count, column_count = queries.shape
    head_count = column_count // HEAD_DIM
    cached_rows = cache_keys.shape[0]
    block_rows = token_count + cached_rows
    scaling = 1.0 / math.sqrt(HEAD_DIM)
    key_block = jnp.concatenate([span_keys, cache_keys], 0)
    value_block = jnp.concatenate([span_values, cache_values], 0)
    piece_keys = lax.all_gather(key_block, "ctx", axis=0, tiled=True)
    piece_values = lax.all_gather(value_block, "ctx", axis=0, tiled=True)
    piece_rows = piece_keys.shape[0]
    index = jnp.arange(piece_rows, dtype=jnp.int32)
    owner = index // block_rows
    within = index % block_rows
    usable = (within < token_count) | (owner * cached_rows + within - token_count < length)
    scores = (
        jnp.einsum(
            "thd,phd->htp",
            queries.reshape(token_count, head_count, HEAD_DIM),
            piece_keys.reshape(piece_rows, head_count, HEAD_DIM),
            preferred_element_type=jnp.float32,
        )
        * scaling
    )
    scores = jnp.where(usable[None, None, :], scores, -1e30)
    peak = jnp.max(scores, axis=2, keepdims=True)
    weights = jnp.where(usable[None, None, :], jnp.exp(scores - peak), 0.0)
    total = jnp.sum(weights, axis=2)
    accum = jnp.einsum(
        "htp,phd->htd",
        weights.astype(jnp.bfloat16),
        piece_values.reshape(piece_rows, head_count, HEAD_DIM),
        preferred_element_type=jnp.float32,
    )
    return (
        (accum / total[:, :, None])
        .transpose(1, 0, 2)
        .reshape(token_count, column_count)
        .astype(jnp.bfloat16)
    )


def attend_by_head(queries, span_keys, span_values, cache_keys, cache_values, length):
    token_count, column_count = queries.shape
    head_count = column_count // HEAD_DIM
    cached_rows = cache_keys.shape[0]
    ctx_count = lax.axis_size("ctx")
    local_heads = head_count // ctx_count
    width = local_heads * HEAD_DIM
    scaling = 1.0 / math.sqrt(HEAD_DIM)
    block_rows = token_count + cached_rows
    packed = jnp.concatenate(
        [queries, span_keys, cache_keys, span_values, cache_values], 0
    )
    packed_rows = packed.shape[0]
    packed = packed.reshape(packed_rows, ctx_count, width)
    got = lax.all_to_all(packed, "ctx", split_axis=1, concat_axis=0, tiled=True)
    got = got.reshape(ctx_count, packed_rows, local_heads, HEAD_DIM)
    query_all = got[:, :token_count].reshape(ctx_count * token_count, local_heads, HEAD_DIM)
    key_all = got[:, token_count : token_count + block_rows].reshape(
        ctx_count * block_rows, local_heads, HEAD_DIM
    )
    value_all = got[:, token_count + block_rows :].reshape(
        ctx_count * block_rows, local_heads, HEAD_DIM
    )
    piece_rows = ctx_count * block_rows
    index = jnp.arange(piece_rows, dtype=jnp.int32)
    owner = index // block_rows
    within = index % block_rows
    usable = (within < token_count) | (owner * cached_rows + within - token_count < length)
    scores = (
        jnp.einsum("thd,phd->htp", query_all, key_all, preferred_element_type=jnp.float32)
        * scaling
    )
    scores = jnp.where(usable[None, None, :], scores, -1e30)
    peak = jnp.max(scores, axis=2, keepdims=True)
    weights = jnp.where(usable[None, None, :], jnp.exp(scores - peak), 0.0)
    total = jnp.sum(weights, axis=2)
    accum = jnp.einsum(
        "htp,phd->thd",
        weights.astype(jnp.bfloat16),
        value_all,
        preferred_element_type=jnp.float32,
    )
    head_out = (accum / total.T[:, :, None]).astype(jnp.bfloat16)
    head_out = head_out.reshape(ctx_count, token_count, width)
    back = lax.all_to_all(head_out, "ctx", split_axis=0, concat_axis=0, tiled=True)
    return back.transpose(1, 0, 2).reshape(token_count, column_count)


def on_device(
    hidden_in,
    queries,
    span_keys,
    span_values,
    cache_keys,
    cache_values,
    cache_lengths,
    slot_request,
    out_weight,
    norm_gain,
    expert_ids,
    expert_gates,
    gate_proj,
    up_proj,
    down_proj,
):
    token_count, feature_width = hidden_in.shape
    column_count = queries.shape[1]
    head_count = column_count // HEAD_DIM
    ctx_count = lax.axis_size("ctx")
    slot_place = lax.axis_index("req")
    slot_count = slot_request.shape[0]
    slot_range = jnp.arange(slot_count, dtype=jnp.int32)
    request = jnp.sum(jnp.where(slot_range == slot_place, slot_request, 0))
    length = jnp.sum(jnp.where(slot_range == request, cache_lengths, 0))
    if head_count % ctx_count == 0:
        attended = attend_by_head(
            queries, span_keys, span_values, cache_keys, cache_values, length
        )
    else:
        attended = attend_gathered(
            queries, span_keys, span_values, cache_keys, cache_values, length
        )
    residual = hidden_in.astype(jnp.float32) + jnp.dot(
        attended, out_weight, preferred_element_type=jnp.float32
    )
    mean_square = jnp.mean(residual * residual, axis=1, keepdims=True)
    normed = (residual * lax.rsqrt(mean_square + 1e-06) * norm_gain).astype(jnp.bfloat16)

    local_experts = gate_proj.shape[0]
    normed_all = lax.all_gather(normed, "ctx", axis=0, tiled=True)
    ids_all = lax.all_gather(expert_ids, "ctx", axis=0, tiled=True)
    gates_all = lax.all_gather(expert_gates, "ctx", axis=0, tiled=True)
    first_expert = lax.axis_index("ctx") * local_experts
    moe = None
    for j in range(local_experts):
        weight = jnp.sum(jnp.where(ids_all == first_expert + j, gates_all, 0.0), axis=1)
        gate_val = jnp.dot(normed_all, gate_proj[j], preferred_element_type=jnp.float32)
        up_val = jnp.dot(normed_all, up_proj[j], preferred_element_type=jnp.float32)
        activated = (jax.nn.silu(gate_val) * up_val).astype(jnp.bfloat16)
        produced = jnp.dot(
            activated, down_proj[j], preferred_element_type=jnp.float32
        ).astype(jnp.bfloat16)
        term = weight[:, None] * produced.astype(jnp.float32)
        moe = term if moe is None else moe + term
    moe_rows = lax.psum_scatter(
        moe.astype(jnp.bfloat16), "ctx", scatter_dimension=0, tiled=True
    )
    final = (residual + moe_rows.astype(jnp.float32)).astype(jnp.bfloat16)

    source_slot = jnp.sum(jnp.where(slot_request == slot_place, slot_range, 0))
    piece = lax.all_gather(final, "req", axis=0, tiled=True)
    piece_rows = piece.shape[0]
    offset = source_slot * token_count
    inside = (offset >= 0) & (offset + token_count <= piece_rows)
    portion = lax.dynamic_slice_in_dim(
        piece, jnp.clip(offset, 0, piece_rows - token_count), token_count, 0
    )
    return jnp.where(inside, portion, jnp.zeros_like(final))


def solution(mesh):
    return jax.shard_map(
        on_device,
        mesh=mesh,
        in_specs=(
            P(("req", "ctx"), None),
            P(("req", "ctx"), None),
            P(("req", "ctx"), None),
            P(("req", "ctx"), None),
            P(("req", "ctx"), None),
            P(("req", "ctx"), None),
            P(),
            P(),
            P(),
            P(),
            P(("req", "ctx"), None),
            P(("req", "ctx"), None),
            P("ctx", None, None),
            P("ctx", None, None),
            P("ctx", None, None),
        ),
        out_specs=P(("req", "ctx"), None),
        check_vma=False,
    )
```

time: 457 us -> 236 us (0.52)
  local copies, waits for them, and re-layouts: 87.9 us -> 9.56 us
  blocking collectives: 98.1 us -> 26.7 us
  waiting for transfers between devices: 183 us -> 134 us
  other arithmetic: 31.6 us -> 10.2 us
    all_to_all x1, blocking collectives: 98.1 us -> 9.35 us  [attend_by_head(): lax.all_to_all(head_out, 'ctx', split_axis=0, concat_axis=0, tiled=True)]
    all_to_all x1, waiting for transfers between devices: 93.7 us -> 18.3 us  [attend_by_head(): got = lax.all_to_all(packed, 'ctx', split_axis=1, concat_axis=0, tiled=True)]
    reduce_scatter x0 -> x1, waiting for transfers between devices: none -> 51.5 us  [on_device(): lax.psum_scatter(moe.astype(jnp.bfloat16), 'ctx', scatter_dimension=0, ti...]
    all_gather x2 -> x1, waiting for transfers between devices: 44.6 us -> 18.9 us  [on_device(): normed_all = lax.all_gather(normed, 'ctx', axis=0, tiled=True)]
    gather x2 -> x0, local copies, waits for them, and re-layouts: 24.3 us -> none  [the longest x1 13.3 us: on_device(): picked = returned[target].reshape(token_count, chosen_count, feature_width)]
    slice x3 -> x5, local copies, waits for them, and re-layouts: 22.4 us -> 1.5 us  [the longest x2 0.84 us: attend_by_head(): got[:, token_count:token_count + block_rows]]
    all_gather x0 -> x2, blocking collectives: none -> 17.3 us  [the longest x1 9.21 us: on_device(): ids_all = lax.all_gather(expert_ids, 'ctx', axis=0, tiled=True)]
    all_gather x2 -> x0, local copies, waits for them, and re-layouts: 15.7 us -> none  [the longest x1 7.95 us: on_device(): piece_values = lax.all_gather(value_block, 'ctx', axis=0, tiled=True)]
  transfers between devices with their start and end apart: 4 -> 4, of which waited for: 4 -> 4; matrix products, arithmetic and copies ran while one was open for 8% -> 1% of each run, Pallas kernels for 0% -> 0%
where the time goes in v1:
time: 236 us; the launch traced here: 235 us
  waiting for transfers between devices  134 us (57%)
  matrix products  35.3 us (15%)
  blocking collectives  26.7 us (11%)
  between operations  14 us (6%)
  other arithmetic  10.2 us (4%)
  local copies, waits for them, and re-layouts  9.56 us (4%)
  starting transfers between devices  5.29 us (2%)
    reduce_scatter x1, waiting for transfers between devices, on_device(): lax.psum_scatter(moe.astype(jnp.bfloat16), 'ctx', scatter_dimension=0, ti...  51.5 us
    all_gather x1, waiting for transfers between devices, on_device(): piece = lax.all_gather(final, 'req', axis=0, tiled=True)  45.4 us
    dot_general x2, matrix products, on_device(): jnp.dot(activated, down_proj[j], preferred_element_type=jnp.float32)  20.6 us
    all_gather x1, waiting for transfers between devices, on_device(): normed_all = lax.all_gather(normed, 'ctx', axis=0, tiled=True)  18.9 us
    all_to_all x1, waiting for transfers between devices, attend_by_head(): got = lax.all_to_all(packed, 'ctx', split_axis=1, concat_axis=0, tiled=True)  18.3 us
    all_to_all x1, blocking collectives, attend_by_head(): lax.all_to_all(head_out, 'ctx', split_axis=0, concat_axis=0, tiled=True)  9.35 us
    all_gather x1, blocking collectives, on_device(): ids_all = lax.all_gather(expert_ids, 'ctx', axis=0, tiled=True)  9.21 us
    dot_general x2, matrix products, on_device(): up_val = jnp.dot(normed_all, up_proj[j], preferred_element_type=jnp.float32)  9.04 us
  transfers between devices with their start and end apart: 4, of which 4 were waited for; matrix products, arithmetic and copies ran while one was open for 1% of the time, Pallas kernels for 0%

profile of v1, /device:TPU:0, one launch (start us, length us, event | category | flops | bytes accessed | tf_op | source)
XLA Modules:
  0.0 235.2 jit_solution(9610870897994373663)
XLA Ops:
  6.5 1.1 copy.17
  7.7 1.1 copy.18
  8.8 1.2 copy.19
  10.0 1.1 copy.20
  11.2 1.2 copy.21
  12.4 2.1 concatenate.3
  14.5 5.2 %all-to-all-start = ((bf16[768,8,128]{0,2,1:T(8,128)(2,1)}), bf16[768,8,128]{0,2,1:T(8,128)(2,1)S(1)}, u32[]{:S(2)}, u32[]{:S(2)}) async-start(bf16[768,8,128]{0,2,1:T(8,128)(2,1)} %bitcast), calls=%async_computation | async-start | bytes 3145728 | tf_op jit(solution)/shard_map/all_to_all | solution.py:67
  19.7 0.7 fusion.54
  20.4 1.3 fusion.56
  21.7 0.6 fusion.53
  22.4 18.3 %all-to-all-done = bf16[768,8,128]{0,2,1:T(8,128)(2,1)S(1)} async-done(((bf16[768,8,128]{0,2,1:T(8,128)(2,1)}), bf16[768,8,128]{0,2,1:T(8,128)(2,1)S(1)}, u32[]{:S(2)}, u32[]{:S(2)}) %all-to-all-start) | async-done | bytes 1572896 | tf_op jit(solution)/shard_map/all_to_all | solution.py:67
  40.7 0.4 fusion.62
  41.2 0.4 copy.22
  41.6 0.2 copy.23
  41.8 0.4 copy.24
  42.3 1.8 fusion
  44.1 2.7 %fusion.1 = f32[1024]{0:T(1024)S(1)} fusion(f32[1024,2560]{1,0:T(8,128)S(1)} %get-tuple-element.12, f32[1024]{0:T(1024)S(1)} %get-tuple-element.11, pred[2560]{0:T(1024)(128)(4,1)S(1)} %fusion.53), kind=kLoop, calls=%fused_computation.4 | loop fusion | flops 13106176 | bytes 10496512 | tf_op jit(solution)/shard_map/reduce_sum | solution.py:88
  46.8 3.0 %fusion.36 = bf16[16,8,8,128]{3,1,2,0:T(8,128)(2,1)S(1)} fusion(bf16[2560,128]{1,0:T(8,128)(2,1)S(1)} %bitcast.66, f32[1024,2560]{1,0:T(8,128)S(1)} %get-tuple-element.12, f32[1024]{0:T(1024)S(1)} %get-tuple-element.11, pred[2560]{0:T(1024)(128)(4,1)S(1)} %fusion.53, f32[1024]{0:T(1024)S(1)} %fusion.1), kind=kOutput, calls=%fused_computation.34 | convolution fusion | flops 684457984 | bytes 11414016 | tf_op jit(solution)/shard_map/htp,phd->thd/dot_general | solution.py:89
  49.9 9.3 %all_to_all.20 = bf16[8,128,128]{1,2,0:T(8,128)(2,1)S(1)} all-to-all(bf16[8,128,128]{1,2,0:T(8,128)(2,1)S(1)} %copy.25), channel_id=1, replica_groups=mesh['req'=4,'ctx'=8] {'ctx'}, dimensions={0} | all-to-all | bytes 524288 | tf_op jit(solution)/shard_map/all_to_all | solution.py:97
  59.3 0.8 multiply_reduce_fusion
  60.1 1.0 multiply_convert_fusion.2
  61.2 8.1 %all_gather.13 = f32[1024,8]{0,1:T(8,128)S(1)} all-gather(f32[128,8]{0,1:T(8,128)S(1)} %copy-done.3), channel_id=1, replica_groups=mesh['req'=4,'ctx'=8] {'ctx'}, dimensions={0}, use_global_device_ids=true | all-gather | bytes 36864 | tf_op jit(solution)/shard_map/all_gather | solution.py:144
  69.3 9.2 %all_gather.12 = s32[1024,8]{0,1:T(8,128)S(1)} all-gather(s32[128,8]{0,1:T(8,128)S(1)} %copy-done.4), channel_id=1, replica_groups=mesh['req'=4,'ctx'=8] {'ctx'}, dimensions={0}, use_global_device_ids=true | all-gather | bytes 36864 | tf_op jit(solution)/shard_map/all_gather | solution.py:143
  78.5 18.9 %all-gather.3.cloned.1.call-done = bf16[1024,2048]{1,0:T(8,128)(2,1)} async-done(((bf16[128,2048]{1,0:T(8,128)(2,1)}), bf16[1024,2048]{1,0:T(8,128)(2,1)}) %all-gather.3.cloned.1.call-update) | async-done | bytes 4194320 | tf_op jit(solution)/shard_map/all_gather | solution.py:142
  97.5 6.7 %fusion.13 = f32[1024,512]{1,0:T(8,128)} fusion(bf16[1024,2048]{1,0:T(8,128)(2,1)} %all-gather.3.cloned.1.call-done, bf16[2,2048,512]{2,1,0:T(8,128)(2,1)} %param.28), kind=kOutput, calls=%fused_computation.16 | convolution fusion | flops 2147483648 | bytes 8388608 | tf_op jit(solution)/shard_map/dot_general | solution.py:150
  104.2 2.3 fusion.7
  106.5 10.7 %fusion.11 = bf16[1024,2048]{1,0:T(8,128)(2,1)} fusion(bf16[2,512,2048]{2,1,0:T(8,128)(2,1)} %param.29, f32[1024,512]{1,0:T(8,128)} %fusion.13, bf16[1024,2048]{1,0:T(8,128)(2,1)} %all-gather.3.cloned.1.call-done, bf16[2,2048,512]{2,1,0:T(8,128)(2,1)} %param.27), kind=kOutput, calls=%fused_computation.14 | convolution fusion | flops 4298113024 | bytes 14680064 | tf_op jit(solution)/shard_map/dot_general | solution.py:152
  117.2 9.9 %add_convert_fusion = bf16[1024,2048]{1,0:T(8,128)(2,1)} fusion(f32[1024]{0:T(1024)S(1)} %get-tuple-element.6, bf16[1024,2048]{1,0:T(8,128)(2,1)} %fusion.11, f32[1024]{0:T(1024)S(1)} %get-tuple-element.5, bf16[2,512,2048]{2,1,0:T(8,128)(2,1)} %param.29, f32[1024,512]{1,0:T(8,128)S(1)} %fusion.7, bf16[1024,2048]{1,0:T(8,128)(2,1)} %all-gather.3.cloned.1.call-done, ...), kind=kOutput, calls=%fused_computation.3 | convolution fusion | flops 4312793088 | bytes 18882560 | tf_op jit(solution)/shard_map/dot_general | solution.py:152
  127.2 51.5 %reduce-scatter.2.cloned.1.call-done = bf16[128,2048]{1,0:T(8,128)(2,1)} async-done(((bf16[1024,2048]{1,0:T(8,128)(2,1)}), bf16[128,2048]{1,0:T(8,128)(2,1)}) %reduce-scatter.2.cloned.1.call-update) | async-done | bytes 524304 | tf_op jit(solution)/shard_map/reduce_scatter | solution.py:157
  178.6 1.9 add_convert_fusion.1
  181.3 45.4 %all-gather.5.cloned.1.call-done = bf16[512,2048]{1,0:T(8,128)(2,1)} async-done(((bf16[128,2048]{1,0:T(8,128)(2,1)}), bf16[512,2048]{1,0:T(8,128)(2,1)}) %all-gather.5.cloned.1.call-update) | async-done | bytes 2097168 | tf_op jit(solution)/shard_map/all_gather | solution.py:163
  226.7 2.0 dynamic-slice_select_fusion
  (29 shorter events, 0.4 us)
Async XLA Ops:
  10.0 9.7 %copy-start.5 = (s32[4]{0:T(128)S(1)}, s32[4]{0:T(128)}, u32[]{:S(2)}) copy-start(s32[4]{0:T(128)} %param.22) | copy-start | bytes 52
  10.0 10.4 %copy-start.8 = (s32[4]{0:T(128)S(1)}, s32[4]{0:T(128)}, u32[]{:S(2)}) copy-start(s32[4]{0:T(128)} %param.21) | copy-start | bytes 52
  14.5 26.2 %all-to-all-start = ((bf16[768,8,128]{0,2,1:T(8,128)(2,1)}), bf16[768,8,128]{0,2,1:T(8,128)(2,1)S(1)}, u32[]{:S(2)}, u32[]{:S(2)}) async-start(bf16[768,8,128]{0,2,1:T(8,128)(2,1)} %bitcast), calls=%async_computation | async-start | bytes 3145728 | tf_op jit(solution)/shard_map/all_to_all | solution.py:67
  19.7 77.8 %all-gather.3.cloned.1.call-start = ((), (), s32[]{:S(2)}) async-start(), calls=%async_computation.3 | async-start | bytes 4718592 | tf_op jit(solution)/shard_map/all_gather | solution.py:142
  46.8 12.5 %copy-start = (bf16[1024,2048]{1,0:T(8,128)(2,1)S(1)}, bf16[1024,2048]{1,0:T(8,128)(2,1)}, u32[]{:S(2)}) copy-start(bf16[1024,2048]{1,0:T(8,128)(2,1)} %param.23) | copy-start | bytes 12582916
  46.8 12.5 %copy-start.1 = (bf16[128,2048]{1,0:T(8,128)(2,1)S(1)}, bf16[128,2048]{1,0:T(8,128)(2,1)}, u32[]{:S(2)}) copy-start(bf16[128,2048]{1,0:T(8,128)(2,1)} %param.15) | copy-start | bytes 1572868
  49.8 10.3 %copy-start.2 = (f32[2048]{0:T(1024)S(1)}, f32[2048]{0:T(1024)}, u32[]{:S(2)}) copy-start(f32[2048]{0:T(1024)} %param.24) | copy-start | bytes 24580
  59.3 1.9 copy-start.3
  59.3 10.0 %copy-start.4 = (s32[128,8]{0,1:T(8,128)S(1)}, s32[128,8]{0,1:T(8,128)}, u32[]{:S(2)}) copy-start(s32[128,8]{0,1:T(8,128)} %param.25) | copy-start | bytes 12292
  61.1 117.5 %reduce-scatter.2.cloned.1.call-start = ((), (), s32[]{:S(2)}) async-start(), calls=%async_computation.4 | async-start | bytes 4718592 | tf_op jit(solution)/shard_map/reduce_scatter | solution.py:157
  97.4 6.7 %copy-start.6 = (bf16[2,2048,512]{2,1,0:T(8,128)(2,1)S(1)}, bf16[2,2048,512]{2,1,0:T(8,128)(2,1)}, u32[]{:S(2)}) copy-start(bf16[2,2048,512]{2,1,0:T(8,128)(2,1)} %param.28) | copy-start | bytes 12582916
  97.4 6.7 %copy-start.7 = (bf16[1024,2048]{1,0:T(8,128)(2,1)S(1)}, bf16[1024,2048]{1,0:T(8,128)(2,1)}, u32[]{:S(2)}) copy-start(bf16[1024,2048]{1,0:T(8,128)(2,1)} %all-gather.3.cloned.1.call-done) | copy-start | bytes 12582916
  127.1 99.6 %all-gather.5.cloned.1.call-start = ((), (), s32[]{:S(2)}) async-start(), calls=%async_computation.5 | async-start | bytes 2621440 | tf_op jit(solution)/shard_map/all_gather | solution.py:163
Sparse Core Ops, SparseCore 0:
  61.2 36.1 all-gather.2
  127.3 51.3 reduce-scatter.1
  180.7 45.9 all-gather.4
